TPU v7x, 32 devices: a whole 2x2x4 slice. The times are simulated.
32 devices in a mesh: seq: 16 (over z, y, core), section: 2 (over x).
Axes of the slice: x: 2, y: 2, z: 4, core: 2. Of those that a mesh axis runs over, the one named last changes fastest.
Arguments:
- inputs: bfloat16 [2, 2048, 2048], P('section', 'seq'), may hold values from -6 to 6
- b_proj: bfloat16 [2, 2048, 128], P('section', 'seq'), may hold values from -0.59765625 to 0.59765625
- c_proj: bfloat16 [2, 2048, 128], P('section', 'seq'), may hold values from -0.59765625 to 0.59765625
- decay_log: float32 [2, 2048, 32], P('section', 'seq'), may hold values from -1 to 0, as said below
- level_weight: float32 [2, 2048, 5, 32], P('section', 'seq'), may hold values from 0.25 to 2
- out_grad: bfloat16 [2, 2048, 2048], P('section', 'seq'), may hold values from -6 to 6
- final_state_grad: float32 [2, 32, 128, 64], P('section'), may hold values from -0.125 to 0.125
Outputs:
- upstream_grad: bfloat16 [2, 2048, 2048], P('section', 'seq')
- b_grad: float32 [2, 2048, 128], P('section', 'seq')
- c_grad: float32 [2, 2048, 128], P('section', 'seq')
- decay_grad: float32 [2, 2048, 32], P('section', 'seq')
- weight_grad: float32 [2, 2048, 5, 32], P('section', 'seq')
Inputs may be any that keep to these rules, and one draw needn't show every extreme that they name: `decay_log`: negative; per head a rate that varies from token to token and from block to block.
All inputs are finite; a program needn't handle non-finite values.
Results may differ from a plain program's by a relative error of at most 0.001.
Values may be sent and summed in bfloat16 or wider, within the bound.
No kernel may reach another device: no remote copies, remote signals or barrier semaphores. Data moves between devices by JAX's collectives and lax.ppermute only.
A program may use at most 128 MiB of HBM per device.

v0:
```python
from functools import partial

import jax
import jax.numpy as jnp
from jax import lax
from jax.sharding import PartitionSpec as P

highest = lax.Precision.HIGHEST


def from_partner(value, axis, apart):
    return lax.ppermute(value, axis, [(i, i ^ 1 << apart) for i in range(lax.axis_size(axis))])


def passed_along(block, axis, distance):
    devices = range(lax.axis_size(axis))
    route = [((i - distance) % len(devices), i) for i in devices]
    return lax.ppermute(block, axis, route)


def block_state(inputs, b_proj, decay_log):
    length, head_count = decay_log.shape
    running = jnp.cumsum(decay_log, axis=0)
    block_total = running[-1]
    factor = jnp.exp(block_total[None, :] - running)
    weighted = inputs.astype(jnp.float32).reshape(length, head_count, -1) * factor[:, :, None]
    state = jnp.einsum("tn,thp->hnp", b_proj.astype(jnp.float32), weighted, precision=highest)
    return (state, block_total)


def block_mixer(inputs, b_proj, c_proj, decay_log, level_weight, carries):
    length, head_count = decay_log.shape
    running = jnp.cumsum(decay_log, axis=0)
    values = inputs.reshape(length, head_count, -1)
    scores = jnp.dot(c_proj, b_proj.T, precision=highest)
    causal = jnp.arange(length)[:, None] >= jnp.arange(length)[None, :]
    spread = running[:, None, :] - running[None, :, :]
    decays = jnp.exp(jnp.where(causal[:, :, None], spread, -jnp.inf))
    mixing = decays * scores[:, :, None]
    local_part = jnp.einsum("tsh,shp->thp", mixing, values, precision=highest)
    result = level_weight[:, 0, :, None] * local_part
    lift = jnp.exp(running)
    for level_index in range(carries.shape[0]):
        reach = jnp.einsum("tn,hnp->thp", c_proj, carries[level_index], precision=highest)
        result = result + (level_weight[:, level_index + 1, :] * lift)[:, :, None] * reach
    return result.reshape(length, -1)


def merge_level(own_state, own_log, prefix_log, peer_state, peer_log, upper):
    carry = jnp.where(upper, jnp.exp(prefix_log)[:, None, None] * peer_state, 0.0)
    joined = jnp.where(
        upper,
        jnp.exp(own_log)[:, None, None] * peer_state + own_state,
        jnp.exp(peer_log)[:, None, None] * own_state + peer_state,
    )
    new_prefix = jnp.where(upper, prefix_log + peer_log, prefix_log)
    return (carry, joined, own_log + peer_log, new_prefix)


def state_spread(b_proj, decay_log, state_grad):
    running = jnp.cumsum(decay_log, axis=0)
    factor = jnp.exp(running[-1][None, :] - running)
    pulled = jnp.einsum("tn,hnp->thp", b_proj.astype(jnp.float32), state_grad, precision=highest)
    return (factor, pulled)


def state_backward(inputs, decay_log, state_grad, total_grad, factor, pulled):
    length, head_count = decay_log.shape
    values = inputs.astype(jnp.float32).reshape(length, head_count, -1)
    weighted = values * factor[:, :, None]
    b_grad = jnp.einsum("thp,hnp->tn", weighted, state_grad, precision=highest)
    log_grad = jnp.sum(values * pulled, axis=2) * factor
    running_grad = (-log_grad).at[-1].add(total_grad + jnp.sum(log_grad, axis=0))
    decay_grad = jnp.cumsum(running_grad[::-1], axis=0)[::-1]
    return (b_grad, decay_grad)


def body(inputs, b_proj, c_proj, decay_log, level_weight, out_grad, final_state_grad):
    own_inputs = inputs[0]
    own_b = b_proj[0]
    own_c = c_proj[0]
    own_decay = decay_log[0]
    own_weight = level_weight[0]
    own_grad = out_grad[0]
    length, head_count = own_decay.shape
    head_size = own_inputs.shape[1] // head_count
    group = 8
    group_width = group * head_size
    levels = lax.axis_size("seq").bit_length() - 1
    position = lax.axis_index("seq")
    state_now, log_now = block_state(own_inputs, own_b, own_decay)
    prefix_now = jnp.zeros_like(log_now)
    saved = []
    carries = []
    for level_index in range(levels):
        upper = position // 2**level_index % 2 == 1
        peer_state, peer_log = from_partner((state_now, log_now), "seq", level_index)
        saved.append((state_now, log_now, prefix_now, peer_state, peer_log, upper))
        carry_now, state_now, log_now, prefix_now = merge_level(
            state_now, log_now, prefix_now, peer_state, peer_log, upper
        )
        carries.append(carry_now)
    all_carries = jnp.stack(carries)
    b_full = own_b.astype(jnp.float32)
    c_full = own_c.astype(jnp.float32)

    def group_step(group_index, buffers):
        input_buf, b_acc, c_acc, decay_buf, weight_buf, carry_buf = buffers
        first_head = group_index * group
        first_col = group_index * group_width
        piece_inputs = lax.dynamic_slice_in_dim(own_inputs, first_col, group_width, 1).astype(
            jnp.float32
        )
        piece_decay = lax.dynamic_slice_in_dim(own_decay, first_head, group, 1)
        piece_weight = lax.dynamic_slice_in_dim(own_weight, first_head, group, 2)
        piece_carry = lax.dynamic_slice_in_dim(all_carries, first_head, group, 1)
        piece_grad = lax.dynamic_slice_in_dim(own_grad, first_col, group_width, 1).astype(
            jnp.float32
        )
        unused, pull = jax.vjp(
            block_mixer, piece_inputs, b_full, c_full, piece_decay, piece_weight, piece_carry
        )
        grads = pull(piece_grad)
        input_buf = lax.dynamic_update_slice_in_dim(input_buf, grads[0], first_col, 1)
        decay_buf = lax.dynamic_update_slice_in_dim(decay_buf, grads[3], first_head, 1)
        weight_buf = lax.dynamic_update_slice_in_dim(weight_buf, grads[4], first_head, 2)
        carry_buf = lax.dynamic_update_slice_in_dim(carry_buf, grads[5], first_head, 1)
        return (input_buf, b_acc + grads[1], c_acc + grads[2], decay_buf, weight_buf, carry_buf)

    start_buffers = (
        jnp.zeros(own_inputs.shape, jnp.float32),
        jnp.zeros(own_b.shape, jnp.float32),
        jnp.zeros(own_c.shape, jnp.float32),
        jnp.zeros(own_decay.shape, jnp.float32),
        jnp.zeros(own_weight.shape, jnp.float32),
        jnp.zeros(all_carries.shape, jnp.float32),
    )
    input_buf, b_acc, c_acc, decay_buf, weight_buf, carry_grads = lax.fori_loop(
        0, head_count // group, group_step, start_buffers
    )
    state_grad = jnp.where(position == 0, final_state_grad[0], 0.0)
    log_grad = jnp.zeros_like(log_now)
    prefix_grad = jnp.zeros_like(log_now)
    for level_index in reversed(range(levels)):
        own_state, own_log, prefix_log, peer_state, peer_log, upper = saved[level_index]
        unused, pull = jax.vjp(
            partial(merge_level, upper=upper), own_state, own_log, prefix_log, peer_state, peer_log
        )
        own_sg, own_lg, prefix_grad, peer_sg, peer_lg = pull(
            (carry_grads[level_index], state_grad, log_grad, prefix_grad)
        )
        back_state, back_log = from_partner((peer_sg, peer_lg), "seq", level_index)
        state_grad = own_sg + back_state
        log_grad = own_lg + back_log
    factor, pulled = state_spread(own_b, own_decay, state_grad)
    b_extra, decay_extra = state_backward(
        own_inputs, own_decay, state_grad, log_grad, factor, pulled
    )
    input_grad = input_buf + (factor[:, :, None] * pulled).reshape(length, -1)
    upstream = passed_along(input_grad.astype(jnp.bfloat16), "section", -1)
    b_grad = b_acc + b_extra
    decay_grad = decay_buf + decay_extra
    return (upstream[None], b_grad[None], c_acc[None], decay_grad[None], weight_buf[None])


def solution(mesh):
    return jax.shard_map(
        body,
        mesh=mesh,
        in_specs=(
            P("section", "seq", None),
            P("section", "seq", None),
            P("section", "seq", None),
            P("section", "seq", None),
            P("section", "seq", None, None),
            P("section", "seq", None),
            P("section", None, None, None),
        ),
        out_specs=(
            P("section", "seq", None),
            P("section", "seq", None),
            P("section", "seq", None),
            P("section", "seq", None),
            P("section", "seq", None, None),
        ),
        check_vma=False,
    )
```

profile of v0, /device:TPU:0, one launch (start us, length us, event | category | flops | bytes accessed | tf_op | source)
XLA Modules:
  0.0 380.0 jit_solution(2617179380145616982)
XLA Ops:
  5.2 2.2 collective-permute-done.1
  7.4 2.9 collective-permute-start.3
  13.3 2.0 collective-permute-start.2
  15.3 22.3 %collective-permute-done.2 = f32[32,128,64]{1,2,0:T(8,128)S(1)} collective-permute-done((f32[32,128,64]{1,2,0:T(8,128)S(1)}, f32[32,128,64]{1,2,0:T(8,128)S(1)}, u32[]{:S(2)}, u32[]{:S(2)}) %collective-permute-start.2) | collective-permute-done | bytes 1048608 | tf_op jit(solution)/shard_map/ppermute | solution.py:12
  39.1 1.9 collective-permute-start.4
  41.2 21.6 %collective-permute-done.5 = f32[32]{0:T(128)S(1)} collective-permute-done((f32[32]{0:T(128)S(1)}, f32[32]{0:T(128)S(1)}, u32[]{:S(2)}, u32[]{:S(2)}) %collective-permute-start.5) | collective-permute-done | bytes 160 | tf_op jit(solution)/shard_map/ppermute | solution.py:12
  63.4 2.9 select_bitcast_fusion.1
  66.3 2.5 collective-permute-start.6
  69.0 2.1 copy.68
  71.9 40.7 %collective-permute-done.6 = f32[32,128,64]{1,2,0:T(8,128)} collective-permute-done((f32[32,128,64]{1,2,0:T(8,128)}, f32[32,128,64]{1,2,0:T(8,128)}, u32[]{:S(2)}, u32[]{:S(2)}) %collective-permute-start.6) | collective-permute-done | bytes 1048608 | tf_op jit(solution)/shard_map/ppermute | solution.py:12
  114.0 3.9 %pad_maximum_fusion = f32[4,32,128,64]{2,3,1,0:T(8,128)} fusion(f32[1,32,128,64]{2,3,1,0:T(8,128)S(1)} %select_bitcast_fusion, f32[1,32,128,64]{2,3,1,0:T(8,128)} %get-tuple-element.465, f32[1,32,128,64]{2,3,1,0:T(8,128)} %get-tuple-element.463, f32[1,32,128,64]{2,3,1,0:T(8,128)S(1)} %copy-done.12), kind=kLoop, calls=%fused_computation.109 | loop fusion | flops 3145728 | bytes 8388608 | tf_op jit(solution)/shard_map/stack | solution.py:103
  120.3 2.5 broadcast_in_dim.201
  122.8 120.8 %while.26 = (s32[]{:T(128)}, f32[128,2048]{1,0:T(8,128)}, f32[128,128]{1,0:T(8,128)S(1)}, f32[128,128]{1,0:T(8,128)}, f32[128,32]{1,0:T(8,128)}, /*index=5*/f32[...) while((s32[]{:T(128)}, f32[128,2048]{1,0:T(8,128)}, ...), condition=%wide.region_12.13_spmd.clone, body=%wide.region_1.12_spmd.clone.sunk | while | flops 1564899328 | bytes 15491688 | solution.py:138
  126.7 2.3 fusion.173
  156.2 2.3 fusion.173
  172.4 1.7 fusion.179
  186.6 2.3 fusion.173
  217.1 2.3 fusion.173
  243.6 2.0 fusion.72
  245.7 2.9 collective-permute-start.7
  248.6 44.6 %collective-permute-done.7 = f32[32]{0:T(128)S(1)} collective-permute-done((f32[32]{0:T(128)}, f32[32]{0:T(128)S(1)}, u32[]{:S(2)}, u32[]{:S(2)}) %collective-permute-start.7) | collective-permute-done | bytes 160 | tf_op jit(solution)/shard_map/ppermute | solution.py:12
  293.3 2.0 fusion.70
  295.4 23.5 %collective-permute-done.9 = f32[32,128,64]{1,2,0:T(8,128)S(1)} collective-permute-done((f32[32,128,64]{1,2,0:T(8,128)S(1)}, f32[32,128,64]{1,2,0:T(8,128)S(1)}, u32[]{:S(2)}, u32[]{:S(2)}) %collective-permute-start.9) | collective-permute-done | bytes 1048608 | tf_op jit(solution)/shard_map/ppermute | solution.py:12
  318.9 3.5 fusion.69
  323.2 22.5 %collective-permute-done.10 = f32[32,128,64]{1,2,0:T(8,128)S(1)} collective-permute-done((f32[32,128,64]{1,2,0:T(8,128)S(1)}, f32[32,128,64]{1,2,0:T(8,128)S(1)}, u32[]{:S(2)}, u32[]{:S(2)}) %collective-permute-start.10) | collective-permute-done | bytes 1048608 | tf_op jit(solution)/shard_map/ppermute | solution.py:12
  346.7 3.0 collective-permute-start.13
  352.8 2.1 collective-permute-done.14
  355.9 2.7 collective-permute-done.15
  358.8 2.1 multiply_reduce_fusion.7
  360.9 2.6 copy.74
  366.9 4.2 %fusion.67 = f32[1,128,128]{2,1,0:T(8,128)} fusion(f32[128,128]{1,0:T(8,128)S(1)} %get-tuple-element.315, f32[128,32,64]{0,2,1:T(8,128)} %get-tuple-element.434, f32[128,32]{0,1:T(8,128)S(1)} %copy-done.20, f32[32,128,64]{1,2,0:T(8,128)} %copy-done.11, f32[32,128,64]{1,2,0:T(8,128)S(1)} %get-tuple-element.428, f32[32]{0:T(128)S(1)} %copy-done.29, pred[]{:T(512)S(6)} %eq.20), kind=kOutput, calls=%fused_computation.114 | convolution fusion | flops 404242432 | bytes 3293313 | tf_op jit(solution)/shard_map/thp,hnp->tn/dot_general | solution.py:71
  371.1 8.1 %collective-permute-done.12 = bf16[128,2048]{1,0:T(8,128)(2,1)S(1)} collective-permute-done((bf16[128,2048]{1,0:T(8,128)(2,1)S(1)}, bf16[128,2048]{1,0:T(8,128)(2,1)S(1)}, u32[]{:S(2)}, u32[]{:S(2)}) %collective-permute-start.12) | collective-permute-done | bytes 524320 | tf_op jit(solution)/shard_map/ppermute | solution.py:18
  (381 shorter events, 133.6 us)
Async XLA Ops:
  2.9 36.0 %copy-start.15 = (f32[128,32]{1,0:T(8,128)}, f32[128,32]{1,0:T(8,128)S(1)}, u32[]{:S(2)}) copy-start(f32[128,32]{1,0:T(8,128)S(1)} %reduce_window_sum.50) | copy-start | bytes 49156
  4.5 7.5 %collective-permute-start = (f32[32,128,64]{1,2,0:T(8,128)S(1)}, f32[32,128,64]{1,2,0:T(8,128)S(1)}, u32[]{:S(2)}, u32[]{:S(2)}) collective-permute-start(f32[32,128,64]{1,2,0:T(8,128)S(1)} %convolution_bitcast_fusion.15), channel_id=1, source_target_pairs={{0,2},{2,0},{4,6},{6,4},{8,10},{10,8},{12,14},{14,12},{16,18},{18,... | collective-permute-start | bytes 3145736 | tf_op jit(solution)/shard_map/ppermute | solution.py:12
  5.1 2.3 collective-permute-start.1
  7.4 4.5 %collective-permute-start.3 = (f32[32]{0:T(128)S(1)}, f32[32]{0:T(128)S(1)}, u32[]{:S(2)}, u32[]{:S(2)}) collective-permute-start(f32[32]{0:T(128)S(1)} %get-tuple-element.444), channel_id=1, source_target_pairs={{0,4},{2,6},{4,0},{6,2},{8,12},{10,14},{12,8},{14,10},{16,20},{18,... | collective-permute-start | bytes 392 | tf_op jit(solution)/shard_map/ppermute | solution.py:12
  11.9 50.8 %copy-start.36 = (f32[32]{0:T(128)}, f32[32]{0:T(128)S(1)}, u32[]{:S(2)}) copy-start(f32[32]{0:T(128)S(1)} %get-tuple-element.440) | copy-start | bytes 388
  11.9 50.8 %copy-start.38 = (f32[32]{0:T(128)}, f32[32]{0:T(128)S(1)}, u32[]{:S(2)}) copy-start(f32[32]{0:T(128)S(1)} %get-tuple-element.474) | copy-start | bytes 388
  12.0 51.4 %copy-start.43 = (f32[32]{0:T(128)}, f32[32]{0:T(128)S(1)}, u32[]{:S(2)}) copy-start(f32[32]{0:T(128)S(1)} %get-tuple-element.439) | copy-start | bytes 388
  12.0 51.4 %copy-start.44 = (f32[32]{0:T(128)}, f32[32]{0:T(128)S(1)}, u32[]{:S(2)}) copy-start(f32[32]{0:T(128)S(1)} %get-tuple-element.473) | copy-start | bytes 388
  13.3 24.3 %collective-permute-start.2 = (f32[32,128,64]{1,2,0:T(8,128)S(1)}, f32[32,128,64]{1,2,0:T(8,128)S(1)}, u32[]{:S(2)}, u32[]{:S(2)}) collective-permute-start(f32[32,128,64]{1,2,0:T(8,128)S(1)} %get-tuple-element.462), channel_id=1, source_target_pairs={{0,4},{2,6},{4,0},{6,2},{8,12},{10,14},{12,8},{14,10},{16,20},{18,... | collective-permute-start | bytes 3145736 | tf_op jit(solution)/shard_map/ppermute | solution.py:12
  39.1 24.3 %collective-permute-start.4 = (f32[32,128,64]{1,2,0:T(8,128)S(1)}, f32[32,128,64]{1,2,0:T(8,128)}, u32[]{:S(2)}, u32[]{:S(2)}) collective-permute-start(f32[32,128,64]{1,2,0:T(8,128)S(1)} %get-tuple-element.464), channel_id=1, source_target_pairs={{0,8},{2,10},{4,12},{6,14},{8,0},{10,2},{12,4},{14,6},{16,24},{18,... | collective-permute-start | bytes 3145736 | tf_op jit(solution)/shard_map/ppermute | solution.py:12
  41.0 21.8 %collective-permute-start.5 = (f32[32]{0:T(128)S(1)}, f32[32]{0:T(128)S(1)}, u32[]{:S(2)}, u32[]{:S(2)}) collective-permute-start(f32[32]{0:T(128)S(1)} %get-tuple-element.474), channel_id=1, source_target_pairs={{0,8},{2,10},{4,12},{6,14},{8,0},{10,2},{12,4},{14,6},{16,24},{18,... | collective-permute-start | bytes 392 | tf_op jit(solution)/shard_map/ppermute | solution.py:12
  62.7 55.2 %copy-start.55 = (f32[32]{0:T(128)}, f32[32]{0:T(128)S(1)}, u32[]{:S(2)}) copy-start(f32[32]{0:T(128)S(1)} %collective-permute-done.5) | copy-start | bytes 388
  63.3 54.6 %copy-start.26 = (f32[32]{0:T(128)}, f32[32]{0:T(128)S(1)}, u32[]{:S(2)}) copy-start(f32[32]{0:T(128)S(1)} %get-tuple-element.471) | copy-start | bytes 388
  63.3 54.6 %copy-start.45 = (f32[32]{0:T(128)}, f32[32]{0:T(128)S(1)}, u32[]{:S(2)}) copy-start(f32[32]{0:T(128)S(1)} %get-tuple-element.470) | copy-start | bytes 388
  66.3 46.3 %collective-permute-start.6 = (f32[32,128,64]{1,2,0:T(8,128)}, f32[32,128,64]{1,2,0:T(8,128)}, u32[]{:S(2)}, u32[]{:S(2)}) collective-permute-start(f32[32,128,64]{1,2,0:T(8,128)} %get-tuple-element.466), channel_id=1, source_target_pairs={{0,16},{2,18},{4,20},{6,22},{8,24},{10,26},{12,28},{14,30},{16,0},... | collective-permute-start | bytes 3145736 | tf_op jit(solution)/shard_map/ppermute | solution.py:12
  68.8 45.1 %copy-start.12 = (f32[1,32,128,64]{2,3,1,0:T(8,128)S(1)}, f32[1,32,128,64]{2,3,1,0:T(8,128)}, u32[]{:S(2)}) copy-start(f32[1,32,128,64]{2,3,1,0:T(8,128)} %get-tuple-element.461) | copy-start | bytes 3145732
  243.6 75.3 %copy-start = (f32[4,32,128,64]{2,3,1,0:T(8,128)S(1)}, f32[4,32,128,64]{2,3,1,0:T(8,128)}, u32[]{:S(2)}) copy-start(f32[4,32,128,64]{2,3,1,0:T(8,128)} %get-tuple-element.314) | copy-start | bytes 12582916
  243.6 75.3 %copy-start.2 = (f32[32,128,64]{1,2,0:T(8,128)S(1)}, f32[32,128,64]{1,2,0:T(8,128)}, u32[]{:S(2)}) copy-start(f32[32,128,64]{1,2,0:T(8,128)} %copy-done.1) | copy-start | bytes 3145732
  243.6 75.3 %copy-start.3 = (f32[1,32,128,64]{2,3,1,0:T(8,128)S(1)}, f32[1,32,128,64]{2,3,1,0:T(8,128)}, u32[]{:S(2)}) copy-start(f32[1,32,128,64]{2,3,1,0:T(8,128)} %param.17) | copy-start | bytes 3145732
  243.6 75.3 %copy-start.5 = (f32[32,128,64]{1,2,0:T(8,128)S(1)}, f32[32,128,64]{1,2,0:T(8,128)}, u32[]{:S(2)}) copy-start(f32[32,128,64]{1,2,0:T(8,128)} %copy-done.4) | copy-start | bytes 3145732
  243.6 75.3 %copy-start.9 = (f32[32,128,64]{1,2,0:T(8,128)S(1)}, f32[32,128,64]{1,2,0:T(8,128)}, u32[]{:S(2)}) copy-start(f32[32,128,64]{1,2,0:T(8,128)} %copy-done.8) | copy-start | bytes 3145732
  243.6 75.3 %copy-start.46 = (f32[32]{0:T(128)S(1)}, f32[32]{0:T(128)}, u32[]{:S(2)}) copy-start(f32[32]{0:T(128)} %copy-done.45) | copy-start | bytes 388
  245.6 47.6 %collective-permute-start.8 = (f32[32,128,64]{1,2,0:T(8,128)S(1)}, f32[32,128,64]{1,2,0:T(8,128)S(1)}, u32[]{:S(2)}, u32[]{:S(2)}) collective-permute-start(f32[32,128,64]{1,2,0:T(8,128)S(1)} %fusion.72), channel_id=1, source_target_pairs={{0,16},{2,18},{4,20},{6,22},{8,24},{10,26},{12,28},{14,30},{16,0},... | collective-permute-start | bytes 3145736 | tf_op jit(solution)/shard_map/ppermute | solution.py:12
  245.7 47.6 %collective-permute-start.7 = (f32[32]{0:T(128)}, f32[32]{0:T(128)S(1)}, u32[]{:S(2)}, u32[]{:S(2)}) collective-permute-start(f32[32]{0:T(128)} %get-tuple-element.438), channel_id=1, source_target_pairs={{0,16},{2,18},{4,20},{6,22},{8,24},{10,26},{12,28},{14,30},{16,0},... | collective-permute-start | bytes 392 | tf_op jit(solution)/shard_map/ppermute | solution.py:12
  295.3 23.6 %collective-permute-start.9 = (f32[32,128,64]{1,2,0:T(8,128)S(1)}, f32[32,128,64]{1,2,0:T(8,128)S(1)}, u32[]{:S(2)}, u32[]{:S(2)}) collective-permute-start(f32[32,128,64]{1,2,0:T(8,128)S(1)} %get-tuple-element.435), channel_id=1, source_target_pairs={{0,8},{2,10},{4,12},{6,14},{8,0},{10,2},{12,4},{14,6},{16,24},{18,... | collective-permute-start | bytes 3145736 | tf_op jit(solution)/shard_map/ppermute | solution.py:12
  322.9 22.7 %collective-permute-start.10 = (f32[32,128,64]{1,2,0:T(8,128)S(1)}, f32[32,128,64]{1,2,0:T(8,128)S(1)}, u32[]{:S(2)}, u32[]{:S(2)}) collective-permute-start(f32[32,128,64]{1,2,0:T(8,128)S(1)} %fusion.68), channel_id=1, source_target_pairs={{0,4},{2,6},{4,0},{6,2},{8,12},{10,14},{12,8},{14,10},{16,20},{18,... | collective-permute-start | bytes 3145736 | tf_op jit(solution)/shard_map/ppermute | solution.py:12
  346.6 12.1 %collective-permute-start.11 = (f32[32,128,64]{1,2,0:T(8,128)S(1)}, f32[32,128,64]{1,2,0:T(8,128)S(1)}, u32[]{:S(2)}, u32[]{:S(2)}) collective-permute-start(f32[32,128,64]{1,2,0:T(8,128)S(1)} %bitcast_add_fusion), channel_id=1, source_target_pairs={{0,2},{2,0},{4,6},{6,4},{8,10},{10,8},{12,14},{14,12},{16,18},{18,... | collective-permute-start | bytes 3145736 | tf_op jit(solution)/shard_map/ppermute | solution.py:12
  346.7 4.6 %collective-permute-start.13 = (f32[32]{0:T(128)S(1)}, f32[32]{0:T(128)S(1)}, u32[]{:S(2)}, u32[]{:S(2)}) collective-permute-start(f32[32]{0:T(128)S(1)} %exponential_multiply_fusion), channel_id=1, source_target_pairs={{0,16},{2,18},{4,20},{6,22},{8,24},{10,26},{12,28},{14,30},{16,0},... | collective-permute-start | bytes 392 | tf_op jit(solution)/shard_map/ppermute | solution.py:12
  351.3 3.6 collective-permute-start.14
  355.0 3.6 collective-permute-start.15
  358.6 7.3 %collective-permute-start.16 = (f32[32]{0:T(128)S(1)}, f32[32]{0:T(128)S(1)}, u32[]{:S(2)}, u32[]{:S(2)}) collective-permute-start(f32[32]{0:T(128)S(1)} %get-tuple-element.426), channel_id=1, source_target_pairs={{0,2},{2,0},{4,6},{6,4},{8,10},{10,8},{12,14},{14,12},{16,18},{18,... | collective-permute-start | bytes 392 | tf_op jit(solution)/shard_map/ppermute | solution.py:12
  364.9 14.4 %collective-permute-start.12 = (bf16[128,2048]{1,0:T(8,128)(2,1)S(1)}, bf16[128,2048]{1,0:T(8,128)(2,1)S(1)}, u32[]{:S(2)}, u32[]{:S(2)}) collective-permute-start(bf16[128,2048]{1,0:T(8,128)(2,1)S(1)} %add_convert_fusion), channel_id=1, source_target_pairs={{1,0},{0,1},{3,2},{2,3},{5,4},{4,5},{7,6},{6,7},{9,8},{8,9},{11,10... | collective-permute-start | bytes 1572872 | tf_op jit(solution)/shard_map/ppermute | solution.py:18
  (54 other events, 1118.3 us)
where the time goes:
time: 383 us; the launch traced here: 380 us
  waiting for transfers between devices  193 us (50%)
  matrix products  89.6 us (23%)
  other arithmetic  43.2 us (11%)
  local copies, waits for them, and re-layouts  31.7 us (8%)
  starting transfers between devices  20 us (5%)
    ppermute x16, waiting for transfers between devices, from_partner(): lax.ppermute(value, axis, [(i, i ^ 1 << apart) for i in range(lax.axis_si...  185 us
    dot_general x48, matrix products, block_mixer(): jnp.einsum('tn,hnp->thp', c_proj, carries[level_index], precision=highest)  52.3 us
    dot_general x12, matrix products, block_mixer(): local_part = jnp.einsum('tsh,shp->thp', mixing, values, precision=highest)  21.7 us
    ppermute x16, starting transfers between devices, from_partner(): lax.ppermute(value, axis, [(i, i ^ 1 << apart) for i in range(lax.axis_si...  19.1 us
    another operation x5, other arithmetic, body(): all_carries = jnp.stack(carries)  10.8 us
    ppermute x1, waiting for transfers between devices, passed_along(): return lax.ppermute(block, axis, route)  8.14 us
    dot_general x9, matrix products, block_mixer(): scores = jnp.dot(c_proj, b_proj.T, precision=highest)  7.85 us
  transfers between devices with their start and end apart: 17, of which 12 were waited for; matrix products, arithmetic and copies ran while one was open for 4% of the time, Pallas kernels for 0%

commit v1 on v0

v1 whole, which is shorter than its diff:
```python
import jax
import jax.numpy as jnp
from jax import lax
from jax.sharding import PartitionSpec as P

highest = lax.Precision.HIGHEST


def from_partner(value, axis, apart):
    return lax.ppermute(value, axis, [(i, i ^ 1 << apart) for i in range(lax.axis_size(axis))])


def passed_along(block, axis, distance):
    devices = range(lax.axis_size(axis))
    route = [((i - distance) % len(devices), i) for i in devices]
    return lax.ppermute(block, axis, route)


def block_state(inputs, b_proj, decay_log):
    length, head_count = decay_log.shape
    running = jnp.cumsum(decay_log, axis=0)
    block_total = running[-1]
    factor = jnp.exp(block_total[None, :] - running)
    weighted = inputs.astype(jnp.float32).reshape(length, head_count, -1) * factor[:, :, None]
    state = jnp.einsum("tn,thp->hnp", b_proj.astype(jnp.float32), weighted, precision=highest)
    return (state, block_total)


def mixer_local(inputs, b_proj, c_proj, decay_log, first_weight):
    length, head_count = decay_log.shape
    running = jnp.cumsum(decay_log, axis=0)
    values = inputs.reshape(length, head_count, -1)
    scores = jnp.dot(c_proj, b_proj.T, precision=highest)
    causal = jnp.arange(length)[:, None] >= jnp.arange(length)[None, :]
    spread = running[:, None, :] - running[None, :, :]
    decays = jnp.exp(jnp.where(causal[:, :, None], spread, -jnp.inf))
    mixing = decays * scores[:, :, None]
    local_part = jnp.einsum("tsh,shp->thp", mixing, values, precision=highest)
    result = first_weight[:, :, None] * local_part
    return result.reshape(length, -1)


def mixer_carry(c_proj, decay_log, upper_weight, carries):
    length, head_count = decay_log.shape
    running = jnp.cumsum(decay_log, axis=0)
    lift = jnp.exp(running)
    result = jnp.zeros((length, head_count, carries.shape[-1]), jnp.float32)
    for level_index in range(carries.shape[0]):
        reach = jnp.einsum("tn,hnp->thp", c_proj, carries[level_index], precision=highest)
        result = result + (upper_weight[:, level_index, :] * lift)[:, :, None] * reach
    return result.reshape(length, -1)


def level_logs(totals, position, levels):
    count = totals.shape[0]
    index = jnp.arange(count)
    own, peer, prefix = [], [], []
    for level_index in range(levels):
        width = 1 << level_index
        base = position // width * width
        other = (position // width ^ 1) * width
        in_own = (index >= base) & (index < base + width)
        in_peer = (index >= other) & (index < other + width)
        in_prefix = (index >= base) & (index < position)
        own.append(jnp.sum(jnp.where(in_own[:, None], totals, 0.0), axis=0))
        peer.append(jnp.sum(jnp.where(in_peer[:, None], totals, 0.0), axis=0))
        prefix.append(jnp.sum(jnp.where(in_prefix[:, None], totals, 0.0), axis=0))
    return (own, peer, prefix)


def halves_usable(state):
    return state.shape[0] % 2 == 0


def exchange_state(state, level_index):
    if level_index == 0 or not halves_usable(state):
        return from_partner(state, "seq", level_index)
    half = state.shape[0] // 2
    core = lax.axis_index("seq") % 2
    mine = lax.dynamic_slice_in_dim(state, core * half, half, 0)
    got = from_partner(mine, "seq", level_index)
    other = from_partner(got, "seq", 0)
    low = jnp.where(core == 0, got, other)
    high = jnp.where(core == 0, other, got)
    return jnp.concatenate([low, high], axis=0)


def exchange_grad(own_grad, peer_grad, level_index):
    if level_index == 0 or not halves_usable(peer_grad):
        return own_grad + from_partner(peer_grad, "seq", level_index)
    half = peer_grad.shape[0] // 2
    core = lax.axis_index("seq") % 2
    mine = lax.dynamic_slice_in_dim(peer_grad, core * half, half, 0)
    theirs = lax.dynamic_slice_in_dim(peer_grad, (1 - core) * half, half, 0)
    summed = mine + from_partner(theirs, "seq", 0)
    back = from_partner(summed, "seq", level_index)
    own_half = lax.dynamic_slice_in_dim(own_grad, core * half, half, 0)
    return lax.dynamic_update_slice_in_dim(own_grad, own_half + back, core * half, 0)


def state_spread(b_proj, decay_log, state_grad):
    running = jnp.cumsum(decay_log, axis=0)
    factor = jnp.exp(running[-1][None, :] - running)
    pulled = jnp.einsum("tn,hnp->thp", b_proj.astype(jnp.float32), state_grad, precision=highest)
    return (factor, pulled)


def state_backward(inputs, decay_log, state_grad, total_grad, factor, pulled):
    length, head_count = decay_log.shape
    values = inputs.astype(jnp.float32).reshape(length, head_count, -1)
    weighted = values * factor[:, :, None]
    b_grad = jnp.einsum("thp,hnp->tn", weighted, state_grad, precision=highest)
    log_grad = jnp.sum(values * pulled, axis=2) * factor
    running_grad = (-log_grad).at[-1].add(total_grad + jnp.sum(log_grad, axis=0))
    decay_grad = jnp.cumsum(running_grad[::-1], axis=0)[::-1]
    return (b_grad, decay_grad)


def body(inputs, b_proj, c_proj, decay_log, level_weight, out_grad, final_state_grad):
    own_inputs = inputs[0]
    own_b = b_proj[0]
    own_c = c_proj[0]
    own_decay = decay_log[0]
    own_weight = level_weight[0]
    own_grad = out_grad[0]
    length, head_count = own_decay.shape
    head_size = own_inputs.shape[1] // head_count
    group = 8
    group_width = group * head_size
    levels = lax.axis_size("seq").bit_length() - 1
    position = lax.axis_index("seq")
    b_full = own_b.astype(jnp.float32)
    c_full = own_c.astype(jnp.float32)
    grad_full = own_grad.astype(jnp.float32)

    state_now, total_now = block_state(own_inputs, own_b, own_decay)
    totals = lax.all_gather(total_now, "seq")
    own_logs, peer_logs, prefixes = level_logs(totals, position, levels)
    uppers = [position // 2**level_index % 2 == 1 for level_index in range(levels)]

    saved_own = []
    saved_peer = []
    carries = []
    for level_index in range(levels):
        upper = uppers[level_index]
        peer_state = exchange_state(state_now, level_index)
        saved_own.append(state_now)
        saved_peer.append(peer_state)
        carries.append(
            jnp.where(upper, jnp.exp(prefixes[level_index])[:, None, None] * peer_state, 0.0)
        )
        if level_index < levels - 1:
            state_now = jnp.where(
                upper,
                jnp.exp(own_logs[level_index])[:, None, None] * peer_state + state_now,
                jnp.exp(peer_logs[level_index])[:, None, None] * state_now + peer_state,
            )
    all_carries = jnp.stack(carries)

    unused, pull_carry = jax.vjp(mixer_carry, c_full, own_decay, own_weight[:, 1:, :], all_carries)
    c_carry, decay_carry, weight_carry, carry_grads = pull_carry(grad_full)

    state_grad = jnp.where(position == 0, final_state_grad[0], 0.0)
    joined_grads = [None] * levels
    for level_index in reversed(range(levels)):
        upper = uppers[level_index]
        joined_grads[level_index] = state_grad
        own_sg = jnp.where(
            upper, state_grad, jnp.exp(peer_logs[level_index])[:, None, None] * state_grad
        )
        peer_sg = jnp.where(
            upper,
            jnp.exp(own_logs[level_index])[:, None, None] * state_grad
            + jnp.exp(prefixes[level_index])[:, None, None] * carry_grads[level_index],
            state_grad,
        )
        state_grad = exchange_grad(own_sg, peer_sg, level_index)

    own_log_grads = []
    peer_log_grads = []
    prefix_grads = []
    for level_index in range(levels):
        upper = uppers[level_index]
        joined_grad = joined_grads[level_index]
        with_peer = jnp.sum(joined_grad * saved_peer[level_index], axis=(1, 2))
        with_own = jnp.sum(joined_grad * saved_own[level_index], axis=(1, 2))
        carry_peer = jnp.sum(carry_grads[level_index] * saved_peer[level_index], axis=(1, 2))
        own_log_grads.append(jnp.where(upper, jnp.exp(own_logs[level_index]) * with_peer, 0.0))
        peer_log_grads.append(jnp.where(upper, 0.0, jnp.exp(peer_logs[level_index]) * with_own))
        prefix_grads.append(jnp.where(upper, jnp.exp(prefixes[level_index]) * carry_peer, 0.0))
    unused, pull_logs = jax.vjp(lambda t: level_logs(t, position, levels), totals)
    (totals_grad,) = pull_logs((own_log_grads, peer_log_grads, prefix_grads))
    totals_grad = lax.psum(totals_grad, "seq")
    log_grad = lax.dynamic_index_in_dim(totals_grad, position, 0, keepdims=False)

    def group_step(group_index, buffers):
        input_buf, b_acc, c_acc, decay_buf, weight_buf = buffers
        first_head = group_index * group
        first_col = group_index * group_width
        piece_inputs = lax.dynamic_slice_in_dim(own_inputs, first_col, group_width, 1).astype(
            jnp.float32
        )
        piece_decay = lax.dynamic_slice_in_dim(own_decay, first_head, group, 1)
        piece_weight = lax.dynamic_slice_in_dim(own_weight[:, 0, :], first_head, group, 1)
        piece_grad = lax.dynamic_slice_in_dim(grad_full, first_col, group_width, 1)
        unused, pull = jax.vjp(mixer_local, piece_inputs, b_full, c_full, piece_decay, piece_weight)
        grads = pull(piece_grad)
        input_buf = lax.dynamic_update_slice_in_dim(input_buf, grads[0], first_col, 1)
        decay_buf = lax.dynamic_update_slice_in_dim(decay_buf, grads[3], first_head, 1)
        weight_buf = lax.dynamic_update_slice_in_dim(weight_buf, grads[4], first_head, 1)
        return (input_buf, b_acc + grads[1], c_acc + grads[2], decay_buf, weight_buf)

    start_buffers = (
        jnp.zeros(own_inputs.shape, jnp.float32),
        jnp.zeros(own_b.shape, jnp.float32),
        jnp.zeros(own_c.shape, jnp.float32),
        jnp.zeros(own_decay.shape, jnp.float32),
        jnp.zeros((length, head_count), jnp.float32),
    )
    input_buf, b_acc, c_acc, decay_buf, weight_first = lax.fori_loop(
        0, head_count // group, group_step, start_buffers
    )

    factor, pulled = state_spread(own_b, own_decay, state_grad)
    b_extra, decay_extra = state_backward(
        own_inputs, own_decay, state_grad, log_grad, factor, pulled
    )
    input_grad = input_buf + (factor[:, :, None] * pulled).reshape(length, -1)
    upstream = passed_along(input_grad.astype(jnp.bfloat16), "section", -1)
    b_grad = b_acc + b_extra
    c_grad = c_acc + c_carry
    decay_grad = decay_buf + decay_carry + decay_extra
    weight_grad = jnp.concatenate([weight_first[:, None, :], weight_carry], axis=1)
    return (upstream[None], b_grad[None], c_grad[None], decay_grad[None], weight_grad[None])


def solution(mesh):
    return jax.shard_map(
        body,
        mesh=mesh,
        in_specs=(
            P("section", "seq", None),
            P("section", "seq", None),
            P("section", "seq", None),
            P("section", "seq", None),
            P("section", "seq", None, None),
            P("section", "seq", None),
            P("section", None, None, None),
        ),
        out_specs=(
            P("section", "seq", None),
            P("section", "seq", None),
            P("section", "seq", None),
            P("section", "seq", None),
            P("section", "seq", None, None),
        ),
        check_vma=False,
    )
```

time: 383 us -> 330 us (0.86)
  waiting for transfers between devices: 193 us -> 109 us
  blocking collectives: 0 us -> 53.3 us
  matrix products: 89.6 us -> 66.1 us
  local copies, waits for them, and re-layouts: 31.7 us -> 49.8 us
  starting transfers between devices: 20 us -> 3.15 us
    ppermute x16 -> x14, waiting for transfers between devices: 185 us -> 109 us  [from_partner(): lax.ppermute(value, axis, [(i, i ^ 1 << apart) for i in range(lax.axis_si...]
    psum x0 -> x1, blocking collectives: none -> 30 us  [body(): totals_grad = lax.psum(totals_grad, 'seq')]
    all_gather x0 -> x1, blocking collectives: none -> 23.3 us  [body(): totals = lax.all_gather(total_now, 'seq')]
    dot_general x69 -> x33, matrix products: 81.9 us -> 59.3 us  [the longest x12 23.2 us: mixer_local(): local_part = jnp.einsum('tsh,shp->thp', mixing, values, precision=highest)]
    ppermute x16 -> x14, starting transfers between devices: 19.1 us -> 1.67 us  [from_partner(): lax.ppermute(value, axis, [(i, i ^ 1 << apart) for i in range(lax.axis_si...]
    select_n x0 -> x21, other arithmetic: none -> 15 us  [the longest x4 7.53 us: body(): jnp.where(upper, jnp.exp(own_logs[level_index])[:, None, None] * state_gr...]
    another operation x14 -> x10, other arithmetic: 16.2 us -> 6.45 us  [the longest x8 5.16 us: mixer_local(): running = jnp.cumsum(decay_log, axis=0)]
    ppermute x1, waiting for transfers between devices: 8.14 us -> 0.01 us  [passed_along(): return lax.ppermute(block, axis, route)]
  transfers between devices with their start and end apart: 17 -> 15, of which waited for: 12 -> 11; matrix products, arithmetic and copies ran while one was open for 4% -> 29% of each run, Pallas kernels for 0% -> 0%
where the time goes in v1:
time: 330 us; the launch traced here: 327 us
  waiting for transfers between devices  109 us (33%)
  matrix products  66.1 us (20%)
  blocking collectives  53.3 us (16%)
  local copies, waits for them, and re-layouts  49.8 us (15%)
  other arithmetic  43.1 us (13%)
    ppermute x14, waiting for transfers between devices, from_partner(): lax.ppermute(value, axis, [(i, i ^ 1 << apart) for i in range(lax.axis_si...  109 us
    psum x1, blocking collectives, body(): totals_grad = lax.psum(totals_grad, 'seq')  30 us
    all_gather x1, blocking collectives, body(): totals = lax.all_gather(total_now, 'seq')  23.3 us
    dot_general x12, matrix products, mixer_local(): local_part = jnp.einsum('tsh,shp->thp', mixing, values, precision=highest)  23.2 us
    dot_general x12, matrix products, mixer_carry(): jnp.einsum('tn,hnp->thp', c_proj, carries[level_index], precision=highest)  22.3 us
    dot_general x9, matrix products, mixer_local(): scores = jnp.dot(c_proj, b_proj.T, precision=highest)  13.8 us
    unnamed x244, local copies, waits for them, and re-layouts  12.7 us
    select_n x4, other arithmetic, body(): jnp.where(upper, jnp.exp(own_logs[level_index])[:, None, None] * state_gr...  7.53 us
  transfers between devices with their start and end apart: 15, of which 11 were waited for; matrix products, arithmetic and copies ran while one was open for 29% of the time, Pallas kernels for 0%

profile of v1, /device:TPU:0, one launch (start us, length us, event | category | flops | bytes accessed | tf_op | source)
XLA Modules:
  0.0 327.4 jit_solution(1720967328978049173)
XLA Ops:
  9.4 23.3 %all-gather = f32[16,1,32]{2,1,0:T(1,128)S(1)} all-gather(f32[1,1,32]{2,1,0:T(1,128)S(1)} %get-tuple-element.459), channel_id=1, replica_groups=mesh['seq'=16,'section'=2] {'seq'}, dimensions={0}, use_global_device_ids=true | all-gather | bytes 2176 | tf_op jit(solution)/shard_map/all_gather | solution.py:137
  33.2 2.1 pad_add_fusion
  35.5 2.0 copy-done
  41.2 24.4 %collective-permute-done.1 = f32[16,128,64]{1,2,0:T(8,128)S(1)} collective-permute-done((f32[16,128,64]{1,2,0:T(8,128)S(1)}, f32[16,128,64]{1,2,0:T(8,128)S(1)}, u32[]{:S(2)}, u32[]{:S(2)}) %collective-permute-start.1) | collective-permute-done | bytes 524320 | tf_op jit(solution)/shard_map/ppermute | solution.py:10
  65.7 2.9 add_select_fusion.5
  68.8 1.9 collective-permute-done.2
  71.0 13.8 %collective-permute-done.3 = f32[16,128,64]{1,2,0:T(8,128)S(1)} collective-permute-done((f32[16,128,64]{1,2,0:T(8,128)S(1)}, f32[16,128,64]{1,2,0:T(8,128)S(1)}, u32[]{:S(2)}, u32[]{:S(2)}) %collective-permute-start.3) | collective-permute-done | bytes 524320 | tf_op jit(solution)/shard_map/ppermute | solution.py:10
  84.8 1.9 add_dynamic-update-slice_fusion.1
  88.7 1.9 collective-permute-done.4
  90.8 13.9 %collective-permute-done.5 = f32[16,128,64]{1,2,0:T(8,128)S(1)} collective-permute-done((f32[16,128,64]{1,2,0:T(8,128)S(1)}, f32[16,128,64]{1,2,0:T(8,128)S(1)}, u32[]{:S(2)}, u32[]{:S(2)}) %collective-permute-start.5) | collective-permute-done | bytes 524320 | tf_op jit(solution)/shard_map/ppermute | solution.py:10
  104.8 2.4 add_select_fusion.3
  110.2 2.1 multiply_reduce_fusion.11
  121.3 12.3 %collective-permute-done.9 = f32[16,128,64]{1,2,0:T(8,128)} collective-permute-done((f32[16,128,64]{1,2,0:T(8,128)}, f32[16,128,64]{1,2,0:T(8,128)}, u32[]{:S(2)}, u32[]{:S(2)}) %collective-permute-start.9) | collective-permute-done | bytes 524320 | tf_op jit(solution)/shard_map/ppermute | solution.py:10
  135.9 65.6 %while.24 = (s32[]{:T(128)}, f32[128,2048]{1,0:T(8,128)}, f32[128,128]{1,0:T(8,128)}, f32[128,128]{1,0:T(8,128)}, f32[128,32]{1,0:T(8,128)}, /*index=5*/f32[128,...) while((s32[]{:T(128)}, f32[128,2048]{1,0:T(8,128)}, ...), condition=%wide.region_7.8_spmd.clone, body=%wide.region_0.7_spmd.clone.sunk | while | flops 354874368 | bytes 5222812 | solution.py:220
  138.0 2.3 fusion.150
  153.7 2.3 fusion.150
  170.3 2.3 fusion.150
  187.0 2.3 fusion.150
  201.5 2.3 broadcast_multiply_fusion
  203.8 2.5 copy.65
  214.3 12.0 %collective-permute-done.11 = f32[16,128,64]{1,2,0:T(8,128)} collective-permute-done((f32[16,128,64]{1,2,0:T(8,128)}, f32[16,128,64]{1,2,0:T(8,128)}, u32[]{:S(2)}, u32[]{:S(2)}) %collective-permute-start.11) | collective-permute-done | bytes 524320 | tf_op jit(solution)/shard_map/ppermute | solution.py:10
  226.9 4.2 %fusion.35 = f32[1,128,128]{2,1,0:T(8,128)} fusion(f32[128,128]{1,0:T(8,128)S(1)} %copy-done.25, f32[128,32,64]{0,2,1:T(8,128)} %get-tuple-element.431, f32[128,32]{0,1:T(8,128)S(1)} %copy-done.39, f32[32,128,64]{1,2,0:T(8,128)} %copy-done.24, f32[32,128,64]{1,2,0:T(8,128)S(1)} %add_dynamic-update-slice_fusion, f32[32]{0:T(128)S(1)} %copy-done.79, pred[]{:T(512)S(6)} %eq.34), kind=kOutput, calls=%fused_computation.73 | convolution fusion | flops 403718144 | bytes 3293313 | tf_op jit(solution)/shard_map/thp,hnp->tn/dot_general | solution.py:112
  238.7 23.9 %collective-permute-done.13 = f32[16,128,64]{1,2,0:T(8,128)} collective-permute-done((f32[16,128,64]{1,2,0:T(8,128)}, f32[16,128,64]{1,2,0:T(8,128)}, u32[]{:S(2)}, u32[]{:S(2)}) %collective-permute-start.13) | collective-permute-done | bytes 524320 | tf_op jit(solution)/shard_map/ppermute | solution.py:10
  262.7 3.6 %convolution_bitcast_fusion.13 = f32[128,128]{1,0:T(8,128)} fusion(f32[32]{0:T(128)S(1)} %copy-done.121, f32[128,32]{0,1:T(8,128)S(1)} %copy-done.49, pred[]{:T(512)S(6)} %eq.35, f32[16,128,64]{1,2,0:T(8,128)} %copy-done.14, f32[16,128,64]{1,2,0:T(8,128)S(1)} %get-tuple-element.437, bf16[128,32,64]{0,2,1:T(8,128)(2,1)S(1)} %bitcast.274), kind=kOutput, calls=%fused_computation.68 | convolution fusion | flops 403963904 | bytes 1654913 | tf_op jit(solution)/shard_map/transpose(jvp(tn,hnp->thp))/dot_general | solution.py:49
  266.4 1.9 fusion.31
  269.1 3.9 %convolution_bitcast_fusion.14 = f32[128,128]{1,0:T(8,128)} fusion(f32[32]{0:T(128)S(1)} %copy-done.119, f32[128,32]{0,1:T(8,128)S(1)} %copy-done.47, pred[]{:T(512)S(6)} %eq.36, f32[16,128,64]{1,2,0:T(8,128)} %copy-done.19, f32[16,128,64]{1,2,0:T(8,128)} %copy-done.17, bf16[128,32,64]{0,2,1:T(8,128)(2,1)S(1)} %bitcast.276), kind=kOutput, calls=%fused_computation.69 | convolution fusion | flops 403963904 | bytes 1654913 | tf_op jit(solution)/shard_map/transpose(jvp(tn,hnp->thp))/dot_general | solution.py:49
  274.5 2.5 fusion.44
  278.6 2.5 multiply_reduce_fusion.10
  281.6 30.0 %psum.7 = f32[16,32]{1,0:T(8,128)S(1)} all-reduce(f32[16,32]{1,0:T(8,128)S(1)} %select_add_fusion), channel_id=1, replica_groups=mesh['seq'=16,'section'=2] {'seq'}, use_global_device_ids=true, to_apply=%region_39.40 | all-reduce | flops 512 | bytes 4096 | tf_op jit(solution)/shard_map/psum | solution.py:193
  319.2 3.0 fusion.37
  322.9 2.6 fusion.40
  325.5 1.9 copy.154
  (461 shorter events, 113.7 us)
Async XLA Ops:
  4.1 108.2 %copy-start.31 = (f32[128,32]{1,0:T(8,128)}, f32[128,32]{1,0:T(8,128)S(1)}, u32[]{:S(2)}) copy-start(f32[128,32]{1,0:T(8,128)S(1)} %reduce_window_sum.63) | copy-start | bytes 49156
  33.1 37.8 %copy-start.94 = (f32[32]{0:T(128)}, f32[32]{0:T(128)S(1)}, u32[]{:S(2)}) copy-start(f32[32]{0:T(128)S(1)} %get-tuple-element.393) | copy-start | bytes 388
  33.1 37.8 %copy-start.98 = (f32[32]{0:T(128)}, f32[32]{0:T(128)S(1)}, u32[]{:S(2)}) copy-start(f32[32]{0:T(128)S(1)} %get-tuple-element.394) | copy-start | bytes 388
  33.1 37.8 %copy-start.96 = (f32[32]{0:T(128)}, f32[32]{0:T(128)S(1)}, u32[]{:S(2)}) copy-start(f32[32]{0:T(128)S(1)} %get-tuple-element.395) | copy-start | bytes 388
  33.1 57.7 %copy-start.100 = (f32[32]{0:T(128)}, f32[32]{0:T(128)S(1)}, u32[]{:S(2)}) copy-start(f32[32]{0:T(128)S(1)} %get-tuple-element.391) | copy-start | bytes 388
  33.1 57.7 %copy-start.104 = (f32[32]{0:T(128)}, f32[32]{0:T(128)S(1)}, u32[]{:S(2)}) copy-start(f32[32]{0:T(128)S(1)} %get-tuple-element.392) | copy-start | bytes 388
  33.1 75.4 %copy-start.102 = (f32[32]{0:T(128)}, f32[32]{0:T(128)S(1)}, u32[]{:S(2)}) copy-start(f32[32]{0:T(128)S(1)} %get-tuple-element.390) | copy-start | bytes 388
  37.8 2.1 collective-permute-start
  41.0 24.6 %collective-permute-start.1 = (f32[16,128,64]{1,2,0:T(8,128)S(1)}, f32[16,128,64]{1,2,0:T(8,128)S(1)}, u32[]{:S(2)}, u32[]{:S(2)}) collective-permute-start(f32[16,128,64]{1,2,0:T(8,128)S(1)} %dynamic-slice_add_fusion.2), channel_id=1, source_target_pairs={{0,16},{2,18},{4,20},{6,22},{8,24},{10,26},{12,28},{14,30},{16,0},... | collective-permute-start | bytes 1572872 | tf_op jit(solution)/shard_map/ppermute | solution.py:10
  68.7 2.0 collective-permute-start.2
  70.8 14.0 %collective-permute-start.3 = (f32[16,128,64]{1,2,0:T(8,128)S(1)}, f32[16,128,64]{1,2,0:T(8,128)S(1)}, u32[]{:S(2)}, u32[]{:S(2)}) collective-permute-start(f32[16,128,64]{1,2,0:T(8,128)S(1)} %dynamic-slice_add_fusion.1), channel_id=1, source_target_pairs={{0,8},{2,10},{4,12},{6,14},{8,0},{10,2},{12,4},{14,6},{16,24},{18,... | collective-permute-start | bytes 1572872 | tf_op jit(solution)/shard_map/ppermute | solution.py:10
  88.6 2.0 collective-permute-start.4
  90.7 14.0 %collective-permute-start.5 = (f32[16,128,64]{1,2,0:T(8,128)S(1)}, f32[16,128,64]{1,2,0:T(8,128)S(1)}, u32[]{:S(2)}, u32[]{:S(2)}) collective-permute-start(f32[16,128,64]{1,2,0:T(8,128)S(1)} %dynamic-slice_add_fusion), channel_id=1, source_target_pairs={{0,4},{2,6},{4,0},{6,2},{8,12},{10,14},{12,8},{14,10},{16,20},{18,... | collective-permute-start | bytes 1572872 | tf_op jit(solution)/shard_map/ppermute | solution.py:10
  107.3 2.9 collective-permute-start.6
  113.7 2.7 collective-permute-start.8
  119.3 14.3 %collective-permute-start.9 = (f32[16,128,64]{1,2,0:T(8,128)}, f32[16,128,64]{1,2,0:T(8,128)}, u32[]{:S(2)}, u32[]{:S(2)}) collective-permute-start(f32[16,128,64]{1,2,0:T(8,128)} %constant_dynamic-slice_fusion.4), channel_id=1, source_target_pairs={{0,4},{2,6},{4,0},{6,2},{8,12},{10,14},{12,8},{14,10},{16,20},{18,... | collective-permute-start | bytes 1572872 | tf_op jit(solution)/shard_map/ppermute | solution.py:10
  133.6 72.8 %collective-permute-start.10 = (f32[16,128,64]{1,2,0:T(8,128)}, f32[16,128,64]{1,2,0:T(8,128)}, u32[]{:S(2)}, u32[]{:S(2)}) collective-permute-start(f32[16,128,64]{1,2,0:T(8,128)} %collective-permute-done.9), channel_id=1, source_target_pairs={{0,2},{2,0},{4,6},{6,4},{8,10},{10,8},{12,14},{14,12},{16,18},{18,... | collective-permute-start | bytes 1572872 | tf_op jit(solution)/shard_map/ppermute | solution.py:10
  207.9 54.8 %copy-start.12 = (f32[16,128,64]{1,2,0:T(8,128)}, f32[16,128,64]{1,2,0:T(8,128)S(1)}, u32[]{:S(2)}) copy-start(f32[16,128,64]{1,2,0:T(8,128)S(1)} %get-tuple-element.437) | copy-start | bytes 1572868
  211.6 14.6 %collective-permute-start.11 = (f32[16,128,64]{1,2,0:T(8,128)}, f32[16,128,64]{1,2,0:T(8,128)}, u32[]{:S(2)}, u32[]{:S(2)}) collective-permute-start(f32[16,128,64]{1,2,0:T(8,128)} %constant_dynamic-slice_fusion.3), channel_id=1, source_target_pairs={{0,8},{2,10},{4,12},{6,14},{8,0},{10,2},{12,4},{14,6},{16,24},{18,... | collective-permute-start | bytes 1572872 | tf_op jit(solution)/shard_map/ppermute | solution.py:10
  212.8 18.3 %collective-permute-start.7 = (bf16[128,2048]{1,0:T(8,128)(2,1)}, bf16[128,2048]{1,0:T(8,128)(2,1)}, u32[]{:S(2)}, u32[]{:S(2)}) collective-permute-start(bf16[128,2048]{1,0:T(8,128)(2,1)} %add_convert_fusion), channel_id=1, source_target_pairs={{1,0},{0,1},{3,2},{2,3},{5,4},{4,5},{7,6},{6,7},{9,8},{8,9},{11,10... | collective-permute-start | bytes 1572872 | tf_op jit(solution)/shard_map/ppermute | solution.py:16
  226.2 6.3 %collective-permute-start.12 = (f32[16,128,64]{1,2,0:T(8,128)}, f32[16,128,64]{1,2,0:T(8,128)}, u32[]{:S(2)}, u32[]{:S(2)}) collective-permute-start(f32[16,128,64]{1,2,0:T(8,128)} %collective-permute-done.11), channel_id=1, source_target_pairs={{0,2},{2,0},{4,6},{6,4},{8,10},{10,8},{12,14},{14,12},{16,18},{18,... | collective-permute-start | bytes 1572872 | tf_op jit(solution)/shard_map/ppermute | solution.py:10
  234.0 32.4 %copy-start.119 = (f32[32]{0:T(128)S(1)}, f32[32]{0:T(128)}, u32[]{:S(2)}) copy-start(f32[32]{0:T(128)} %copy-done.118) | copy-start | bytes 388
  235.3 33.8 %copy-start.47 = (f32[128,32]{0,1:T(8,128)S(1)}, f32[128,32]{0,1:T(8,128)}, u32[]{:S(2)}) copy-start(f32[128,32]{0,1:T(8,128)} %copy-done.46) | copy-start | bytes 49156
  236.1 26.5 %collective-permute-start.13 = (f32[16,128,64]{1,2,0:T(8,128)}, f32[16,128,64]{1,2,0:T(8,128)}, u32[]{:S(2)}, u32[]{:S(2)}) collective-permute-start(f32[16,128,64]{1,2,0:T(8,128)} %constant_dynamic-slice_fusion.9), channel_id=1, source_target_pairs={{0,16},{2,18},{4,20},{6,22},{8,24},{10,26},{12,28},{14,30},{16,0},... | collective-permute-start | bytes 1572872 | tf_op jit(solution)/shard_map/ppermute | solution.py:10
  262.7 10.4 %collective-permute-start.14 = (f32[16,128,64]{1,2,0:T(8,128)}, f32[16,128,64]{1,2,0:T(8,128)}, u32[]{:S(2)}, u32[]{:S(2)}) collective-permute-start(f32[16,128,64]{1,2,0:T(8,128)} %collective-permute-done.13), channel_id=1, source_target_pairs={{0,2},{2,0},{4,6},{6,4},{8,10},{10,8},{12,14},{14,12},{16,18},{18,... | collective-permute-start | bytes 1572872 | tf_op jit(solution)/shard_map/ppermute | solution.py:10
  278.6 36.9 %copy-start.28 = (f32[1,128,5,32]{3,1,2,0:T(8,128)S(1)}, f32[1,128,5,32]{3,1,2,0:T(8,128)}, u32[]{:S(2)}) copy-start(f32[1,128,5,32]{3,1,2,0:T(8,128)} %copy-done.27) | copy-start | bytes 245764
  278.6 36.9 %copy-start.32 = (f32[128,32]{1,0:T(8,128)S(1)}, f32[128,32]{1,0:T(8,128)}, u32[]{:S(2)}) copy-start(f32[128,32]{1,0:T(8,128)} %copy-done.31) | copy-start | bytes 49156
  278.6 40.6 %copy-start.45 = (f32[128,32]{0,1:T(8,128)S(1)}, f32[128,32]{0,1:T(8,128)}, u32[]{:S(2)}) copy-start(f32[128,32]{0,1:T(8,128)} %copy-done.44) | copy-start | bytes 49156
  281.1 41.1 %copy-start.50 = (f32[128,32]{0,1:T(8,128)S(1)}, f32[128,32]{0,1:T(8,128)}, u32[]{:S(2)}) copy-start(f32[128,32]{0,1:T(8,128)} %get-tuple-element.278) | copy-start | bytes 49156
  281.1 41.8 %copy-start.26 = (f32[128,128]{1,0:T(8,128)S(1)}, f32[128,128]{1,0:T(8,128)}, u32[]{:S(2)}) copy-start(f32[128,128]{1,0:T(8,128)} %get-tuple-element.276) | copy-start | bytes 196612
  281.1 41.8 %copy-start.41 = (f32[128,32]{0,1:T(8,128)S(1)}, f32[128,32]{0,1:T(8,128)}, u32[]{:S(2)}) copy-start(f32[128,32]{0,1:T(8,128)} %copy-done.40) | copy-start | bytes 49156
  281.1 41.8 %copy-start.53 = (f32[32]{0:T(128)S(1)}, f32[32]{0:T(128)}, u32[]{:S(2)}) copy-start(f32[32]{0:T(128)} %copy-done.51) | copy-start | bytes 388
  (114 other events, 840.0 us)

commit v2 on v1

--- a/solution.py
+++ b/solution.py
@@ -66,6 +66,26 @@
         peer.append(jnp.sum(jnp.where(in_peer[:, None], totals, 0.0), axis=0))
         prefix.append(jnp.sum(jnp.where(in_prefix[:, None], totals, 0.0), axis=0))
     return (own, peer, prefix)
+
+
+def gather_blocks(value, axis):
+    position = lax.axis_index(axis)
+    blocks = value[None]
+    for level_index in range(lax.axis_size(axis).bit_length() - 1):
+        other = from_partner(blocks, axis, level_index)
+        upper = position // 2**level_index % 2 == 1
+        blocks = jnp.where(
+            upper,
+            jnp.concatenate([other, blocks], axis=0),
+            jnp.concatenate([blocks, other], axis=0),
+        )
+    return blocks
+
+
+def sum_over(value, axis):
+    for level_index in range(lax.axis_size(axis).bit_length() - 1):
+        value = value + from_partner(value, axis, level_index)
+    return value
 
 
 def halves_usable(state):
@@ -134,20 +154,30 @@
     grad_full = own_grad.astype(jnp.float32)
 
     state_now, total_now = block_state(own_inputs, own_b, own_decay)
-    totals = lax.all_gather(total_now, "seq")
+    totals = gather_blocks(total_now, "seq")
     own_logs, peer_logs, prefixes = level_logs(totals, position, levels)
     uppers = [position // 2**level_index % 2 == 1 for level_index in range(levels)]
 
-    saved_own = []
-    saved_peer = []
-    carries = []
-    for level_index in range(levels):
+    unused, pull_carry = jax.vjp(
+        mixer_carry, c_full, own_decay, own_weight[:, 1:, :],
+        jnp.zeros((levels,) + state_now.shape, jnp.float32),
+    )
+    carry_grads = pull_carry(grad_full)[3]
+
+    saved_own = [None] * levels
+    saved_peer = [None] * levels
+    carries = [None] * levels
+    joined_grads = [None] * levels
+    state_grad = jnp.where(position == 0, final_state_grad[0], 0.0)
+    for step in range(levels):
+        state_now, state_grad = lax.optimization_barrier((state_now, state_grad))
+        level_index = step
         upper = uppers[level_index]
         peer_state = exchange_state(state_now, level_index)
-        saved_own.append(state_now)
-        saved_peer.append(peer_state)
-        carries.append(
-            jnp.where(upper, jnp.exp(prefixes[level_index])[:, None, None] * peer_state, 0.0)
+        saved_own[level_index] = state_now
+        saved_peer[level_index] = peer_state
+        carries[level_index] = jnp.where(
+            upper, jnp.exp(prefixes[level_index])[:, None, None] * peer_state, 0.0
         )
         if level_index < levels - 1:
             state_now = jnp.where(
@@ -155,14 +185,7 @@
                 jnp.exp(own_logs[level_index])[:, None, None] * peer_state + state_now,
                 jnp.exp(peer_logs[level_index])[:, None, None] * state_now + peer_state,
             )
-    all_carries = jnp.stack(carries)
-
-    unused, pull_carry = jax.vjp(mixer_carry, c_full, own_decay, own_weight[:, 1:, :], all_carries)
-    c_carry, decay_carry, weight_carry, carry_grads = pull_carry(grad_full)
-
-    state_grad = jnp.where(position == 0, final_state_grad[0], 0.0)
-    joined_grads = [None] * levels
-    for level_index in reversed(range(levels)):
+        level_index = levels - 1 - step
         upper = uppers[level_index]
         joined_grads[level_index] = state_grad
         own_sg = jnp.where(
@@ -175,6 +198,10 @@
             state_grad,
         )
         state_grad = exchange_grad(own_sg, peer_sg, level_index)
+    all_carries = jnp.stack(carries)
+
+    unused, pull_carry = jax.vjp(mixer_carry, c_full, own_decay, own_weight[:, 1:, :], all_carries)
+    c_carry, decay_carry, weight_carry, unused_grads = pull_carry(grad_full)
 
     own_log_grads = []
     peer_log_grads = []
@@ -190,7 +217,7 @@
         prefix_grads.append(jnp.where(upper, jnp.exp(prefixes[level_index]) * carry_peer, 0.0))
     unused, pull_logs = jax.vjp(lambda t: level_logs(t, position, levels), totals)
     (totals_grad,) = pull_logs((own_log_grads, peer_log_grads, prefix_grads))
-    totals_grad = lax.psum(totals_grad, "seq")
+    totals_grad = sum_over(totals_grad, "seq")
     log_grad = lax.dynamic_index_in_dim(totals_grad, position, 0, keepdims=False)
 
     def group_step(group_index, buffers):

time: 330 us -> 276 us (0.84)
  blocking collectives: 53.3 us -> 0 us
  waiting for transfers between devices: 109 us -> 74.9 us
  starting transfers between devices: 3.15 us -> 25 us
  other arithmetic: 43.1 us -> 54 us
    ppermute x14 -> x22, waiting for transfers between devices: 109 us -> 69.5 us  [from_partner(): lax.ppermute(value, axis, [(i, i ^ 1 << apart) for i in range(lax.axis_si...]
    psum x1 -> x0, blocking collectives: 30 us -> none  [body(): totals_grad = lax.psum(totals_grad, 'seq')]
    all_gather x1 -> x0, blocking collectives: 23.3 us -> none  [body(): totals = lax.all_gather(total_now, 'seq')]
    ppermute x14 -> x22, starting transfers between devices: 1.67 us -> 22.7 us  [from_partner(): lax.ppermute(value, axis, [(i, i ^ 1 << apart) for i in range(lax.axis_si...]
    reduce_sum x2, other arithmetic: 3.55 us -> 9.1 us  [body(): with_own = jnp.sum(joined_grad * saved_own[level_index], axis=(1, 2))]
    ppermute x1, waiting for transfers between devices: 0.01 us -> 5.46 us  [passed_along(): return lax.ppermute(block, axis, route)]
    dynamic_slice x4, local copies, waits for them, and re-layouts: 0.31 us -> 3.66 us  [group_step(): piece_decay = lax.dynamic_slice_in_dim(own_decay, first_head, group, 1)]
    unnamed x244 -> x218, local copies, waits for them, and re-layouts: 12.7 us -> 11.5 us
  transfers between devices with their start and end apart: 15 -> 23, of which waited for: 11 -> 11; matrix products, arithmetic and copies ran while one was open for 29% -> 52% of each run, Pallas kernels for 0% -> 0%
where the time goes in v2:
time: 276 us; the launch traced here: 273 us
  waiting for transfers between devices  74.9 us (27%)
  matrix products  68.2 us (25%)
  other arithmetic  54 us (20%)
  local copies, waits for them, and re-layouts  48.1 us (17%)
  starting transfers between devices  25 us (9%)
    ppermute x22, waiting for transfers between devices, from_partner(): lax.ppermute(value, axis, [(i, i ^ 1 << apart) for i in range(lax.axis_si...  69.5 us
    dot_general x12, matrix products, mixer_local(): local_part = jnp.einsum('tsh,shp->thp', mixing, values, precision=highest)  23.2 us
    ppermute x22, starting transfers between devices, from_partner(): lax.ppermute(value, axis, [(i, i ^ 1 << apart) for i in range(lax.axis_si...  22.7 us
    dot_general x12, matrix products, mixer_carry(): jnp.einsum('tn,hnp->thp', c_proj, carries[level_index], precision=highest)  21.4 us
    dot_general x9, matrix products, mixer_local(): scores = jnp.dot(c_proj, b_proj.T, precision=highest)  14.7 us
    unnamed x218, local copies, waits for them, and re-layouts  11.5 us
    reduce_sum x2, other arithmetic, body(): with_own = jnp.sum(joined_grad * saved_own[level_index], axis=(1, 2))  9.1 us
    dynamic_update_slice x8, local copies, waits for them, and re-layouts, group_step(): lax.dynamic_update_slice_in_dim(input_buf, grads[0], first_col, 1)  7.3 us
  transfers between devices with their start and end apart: 23, of which 11 were waited for; matrix products, arithmetic and copies ran while one was open for 52% of the time, Pallas kernels for 0%

profile of v2, /device:TPU:0, one launch (start us, length us, event | category | flops | bytes accessed | tf_op | source)
XLA Modules:
  0.0 272.8 jit_solution(3182769084531241736)
XLA Ops:
  8.3 2.7 select_bitcast_fusion
  15.6 2.3 pad_add_fusion
  19.6 2.0 collective-permute-done.1
  23.3 2.0 collective-permute-done.2
  25.3 2.7 collective-permute-start.3
  30.7 2.9 %add_select_fusion.5 = (f32[32,128,64]{1,2,0:T(8,128)S(1)}, f32[32,128,64]{1,2,0:T(8,128)}) fusion(f32[32,128,64]{1,2,0:T(8,128)} %select_bitcast_fusion, f32[4,32,128,64]{2,3,1,0:T(8,128)} %pad_add_fusion, f32[32]{0:T(128)S(1)} %exp.166, f32[32]{0:T(128)S(1)} %exp.165, pred[]{:T(512)S(6)} %eq.44, f32[32]{0:T(128)S(1)} %exp.164), kind=kLoop, calls=%fused_computation.116 | loop fusion | flops 1572864 | bytes 4194689 | tf_op jit(solution)/shard_map/jit(_where)/select_n | solution.py:194
  35.4 2.2 collective-permute-done.5
  39.0 2.7 collective-permute-start.6
  43.3 21.8 %collective-permute-done.6 = f32[16,128,64]{1,2,0:T(8,128)S(1)} collective-permute-done((f32[16,128,64]{1,2,0:T(8,128)S(1)}, f32[16,128,64]{1,2,0:T(8,128)S(1)}, u32[]{:S(2)}, u32[]{:S(2)}) %collective-permute-start.6) | collective-permute-done | bytes 524320 | tf_op jit(solution)/shard_map/ppermute | solution.py:10
  66.9 2.5 add_select_fusion.3
  71.2 7.3 %collective-permute-done.7 = f32[16,128,64]{1,2,0:T(8,128)} collective-permute-done((f32[16,128,64]{1,2,0:T(8,128)S(1)}, f32[16,128,64]{1,2,0:T(8,128)}, u32[]{:S(2)}, u32[]{:S(2)}) %collective-permute-start.7) | collective-permute-done | bytes 524320 | tf_op jit(solution)/shard_map/ppermute | solution.py:10
  83.1 11.3 %collective-permute-done.10 = f32[16,128,64]{1,2,0:T(8,128)S(1)} collective-permute-done((f32[16,128,64]{1,2,0:T(8,128)S(1)}, f32[16,128,64]{1,2,0:T(8,128)S(1)}, u32[]{:S(2)}, u32[]{:S(2)}) %collective-permute-start.10) | collective-permute-done | bytes 524320 | tf_op jit(solution)/shard_map/ppermute | solution.py:10
  100.5 7.7 %collective-permute-done.11 = f32[16,128,64]{1,2,0:T(8,128)} collective-permute-done((f32[16,128,64]{1,2,0:T(8,128)S(1)}, f32[16,128,64]{1,2,0:T(8,128)}, u32[]{:S(2)}, u32[]{:S(2)}) %collective-permute-start.11) | collective-permute-done | bytes 524320 | tf_op jit(solution)/shard_map/ppermute | solution.py:10
  114.2 11.2 %collective-permute-done.14 = f32[16,128,64]{1,2,0:T(8,128)S(1)} collective-permute-done((f32[16,128,64]{1,2,0:T(8,128)S(1)}, f32[16,128,64]{1,2,0:T(8,128)S(1)}, u32[]{:S(2)}, u32[]{:S(2)}) %collective-permute-start.14) | collective-permute-done | bytes 524320 | tf_op jit(solution)/shard_map/ppermute | solution.py:10
  126.3 3.4 %collective-permute-start.17 = (f32[16,128,64]{1,2,0:T(8,128)}, f32[16,128,64]{1,2,0:T(8,128)}, u32[]{:S(2)}, u32[]{:S(2)}) collective-permute-start(f32[16,128,64]{1,2,0:T(8,128)} %constant_dynamic-slice_fusion.3), channel_id=1, source_target_pairs={{0,16},{2,18},{4,20},{6,22},{8,24},{10,26},{12,28},{14,30},{16,0},... | collective-permute-start | bytes 1572872 | tf_op jit(solution)/shard_map/ppermute | solution.py:10
  132.0 69.8 %while.24 = (s32[]{:T(128)}, f32[128,2048]{1,0:T(8,128)}, f32[128,128]{1,0:T(8,128)}, f32[128,128]{1,0:T(8,128)}, f32[128,32]{1,0:T(8,128)}, /*index=5*/f32[128,...) while((s32[]{:T(128)}, f32[128,2048]{1,0:T(8,128)}, ...), condition=%wide.region_7.8_spmd.clone, body=%wide.region_0.7_spmd.clone.sunk | while | flops 354874368 | bytes 5222804 | solution.py:247
  134.9 2.3 fusion.151
  152.3 2.3 fusion.151
  169.8 2.3 fusion.151
  187.2 2.3 fusion.151
  204.0 3.8 %convolution_bitcast_fusion.13 = f32[128,128]{1,0:T(8,128)} fusion(f32[32]{0:T(128)} %copy-done.106, f32[128,32]{0,1:T(8,128)} %copy-done.45, pred[]{:T(512)S(6)} %eq.45, f32[16,128,64]{1,2,0:T(8,128)} %copy-done.11, f32[16,128,64]{1,2,0:T(8,128)} %copy-done.10, bf16[128,32,64]{0,2,1:T(8,128)(2,1)S(1)} %bitcast.258), kind=kOutput, calls=%fused_computation.68 | convolution fusion | flops 403963904 | bytes 1654913 | tf_op jit(solution)/shard_map/transpose(jvp(tn,hnp->thp))/dot_general | solution.py:49
  209.9 3.8 %convolution_bitcast_fusion.14 = f32[128,128]{1,0:T(8,128)} fusion(f32[32]{0:T(128)S(1)} %copy-done.105, f32[128,32]{0,1:T(8,128)S(1)} %copy-done.44, pred[]{:T(512)S(6)} %eq.43, f32[16,128,64]{1,2,0:T(8,128)} %copy-done.13, f32[16,128,64]{1,2,0:T(8,128)} %copy-done.12, bf16[128,32,64]{0,2,1:T(8,128)(2,1)S(1)} %bitcast.260), kind=kOutput, calls=%fused_computation.69 | convolution fusion | flops 403963904 | bytes 1654913 | tf_op jit(solution)/shard_map/transpose(jvp(tn,hnp->thp))/dot_general | solution.py:49
  216.8 6.1 %multiply_reduce_fusion.11 = (f32[32]{0:T(128)S(1)}, f32[32]{0:T(128)S(1)}, f32[32]{0:T(128)S(1)}, f32[32]{0:T(128)S(1)}, f32[32]{0:T(128)S(1)}, /*index=5*/f32[...) fusion(f32[32,128,64]{1,2,0:T(8,128)} %select_bitcast_fusion, ...), kind=kLoop, calls=%fused_computation.98 | loop fusion | flops 6028992 | bytes 14681344 | tf_op jit(solution)/shard_map/reduce_sum | solution.py:213
  229.9 3.0 %multiply_reduce_fusion.2 = (f32[32]{0:T(128)S(1)}, f32[32]{0:T(128)S(1)}, f32[32,128,64]{1,2,0:T(8,128)}) fusion(f32[32,128,64]{1,2,0:T(8,128)S(1)} %add_dynamic-update-slice_fusion, f32[32,128,64]{1,2,0:T(8,128)} %copy-done.7, f32[32,128,64]{1,2,0:T(8,128)S(1)} %collective-permute-done.4, f32[4,32,128,64]{2,3,1,0:T(8,128)} %pad_add_fusion, ...), kind=kLoop, calls=%fused_computation.89 | loop fusion | flops 2097088 | bytes 5243393 | tf_op jit(solution)/shard_map/reduce_sum | solution.py:213
  235.7 2.5 fusion.37
  238.9 3.5 %fusion.40 = f32[1,128,128]{2,1,0:T(8,128)} fusion(f32[128,128]{1,0:T(8,128)S(1)} %copy-done.19, f32[128,128]{1,0:T(8,128)S(1)} %fusion.37, f32[32,128,64]{1,2,0:T(8,128)S(1)} %collective-permute-done.4, f32[32]{0:T(128)} %copy-done.72, f32[128,32]{0,1:T(8,128)S(1)} %copy-done.38, pred[]{:T(512)S(6)} %eq.42, bf16[128,32,64]{0,2,1:T(8,128)(2,1)S(1)} %bitcast.264), kind=kOutput, calls=%fused_computation.78 | convolution fusion | flops 403734528 | bytes 1785985 | tf_op jit(solution)/shard_map/transpose(jvp(tn,hnp->thp))/dot_general | solution.py:49
  244.5 2.0 collective-permute-done.20
  251.6 3.4 %multiply_reduce_fusion.13 = (f32[128,32]{0,1:T(8,128)S(1)}, f32[128,32,64]{0,2,1:T(8,128)}, f32[128,32,64]{0,2,1:T(8,128)}) fusion(bf16[128,32,64]{0,2,1:T(8,128)(2,1)S(1)} %bitcast.266, f32[128,32]{0,1:T(8,128)S(1)} %copy-done.35, bf16[1,128,128]{2,1,0:T(8,128)(2,1)S(1)} %copy-done.33, f32[32,128,64]{1,2,0:T(8,128)} %collective-permute-done.15, ...), kind=kOutput, calls=%fused_computation.100 | convolution fusion | flops 404484096 | bytes 4784257 | tf_op jit(solution)/shard_map/tn,hnp->thp/dot_general | solution.py:124
  255.1 2.6 copy.64
  259.1 2.3 collective-permute-start.16
  262.4 4.2 %fusion.35 = f32[1,128,128]{2,1,0:T(8,128)} fusion(f32[128,128]{1,0:T(8,128)S(1)} %copy-done.18, f32[128,32,64]{0,2,1:T(8,128)} %get-tuple-element.445, f32[128,32]{0,1:T(8,128)S(1)} %copy-done.35, f32[32,128,64]{1,2,0:T(8,128)} %collective-permute-done.15, f32[32,128,64]{1,2,0:T(8,128)S(1)} %add_dynamic-update-slice_fusion, f32[32]{0:T(128)S(1)} %copy-done.86, ...), kind=kOutput, calls=%fused_computation.73 | convolution fusion | flops 403718144 | bytes 3293313 | tf_op jit(solution)/shard_map/thp,hnp->tn/dot_general | solution.py:132
  266.5 5.5 %collective-permute-done.16 = bf16[128,2048]{1,0:T(8,128)(2,1)S(1)} collective-permute-done((bf16[128,2048]{1,0:T(8,128)(2,1)S(1)}, bf16[128,2048]{1,0:T(8,128)(2,1)S(1)}, u32[]{:S(2)}, u32[]{:S(2)}) %collective-permute-start.16) | collective-permute-done | bytes 524320 | tf_op jit(solution)/shard_map/ppermute | solution.py:16
  (452 shorter events, 133.8 us)
Async XLA Ops:
  3.1 14.8 %collective-permute-start = (f32[1,32]{1,0:T(1,128)S(1)}, f32[1,32]{1,0:T(1,128)S(1)}, u32[]{:S(2)}, u32[]{:S(2)}) collective-permute-start(f32[1,32]{1,0:T(1,128)S(1)} %get-tuple-element.484), channel_id=1, source_target_pairs={{0,2},{2,0},{4,6},{6,4},{8,10},{10,8},{12,14},{14,12},{16,18},{18,... | collective-permute-start | bytes 392 | tf_op jit(solution)/shard_map/ppermute | solution.py:10
  11.0 30.7 %collective-permute-start.4 = (f32[32,128,64]{1,2,0:T(8,128)S(1)}, f32[32,128,64]{1,2,0:T(8,128)S(1)}, u32[]{:S(2)}, u32[]{:S(2)}) collective-permute-start(f32[32,128,64]{1,2,0:T(8,128)S(1)} %convolution_bitcast_fusion.11), channel_id=1, source_target_pairs={{0,2},{2,0},{4,6},{6,4},{8,10},{10,8},{12,14},{14,12},{16,18},{18,... | collective-permute-start | bytes 3145736 | tf_op jit(solution)/shard_map/ppermute | solution.py:10
  11.0 19.5 %copy-start.58 = (pred[16]{0:T(512)(128)(4,1)}, pred[16]{0:T(512)(128)(4,1)S(1)}, u32[]{:S(2)}) copy-start(pred[16]{0:T(512)(128)(4,1)S(1)} %get-tuple-element.497) | copy-start | bytes 52
  17.9 3.6 %collective-permute-start.1 = (f32[2,32]{1,0:T(2,128)S(1)}, f32[2,32]{1,0:T(2,128)S(1)}, u32[]{:S(2)}, u32[]{:S(2)}) collective-permute-start(f32[2,32]{1,0:T(2,128)S(1)} %maximum_select_fusion.3), channel_id=1, source_target_pairs={{0,4},{2,6},{4,0},{6,2},{8,12},{10,14},{12,8},{14,10},{16,20},{18,... | collective-permute-start | bytes 776 | tf_op jit(solution)/shard_map/ppermute | solution.py:10
  21.6 3.7 %collective-permute-start.2 = (f32[4,32]{1,0:T(4,128)S(1)}, f32[4,32]{1,0:T(4,128)S(1)}, u32[]{:S(2)}, u32[]{:S(2)}) collective-permute-start(f32[4,32]{1,0:T(4,128)S(1)} %maximum_select_fusion.2), channel_id=1, source_target_pairs={{0,8},{2,10},{4,12},{6,14},{8,0},{10,2},{12,4},{14,6},{16,24},{18,... | collective-permute-start | bytes 1544 | tf_op jit(solution)/shard_map/ppermute | solution.py:10
  25.3 4.6 %collective-permute-start.3 = (f32[8,32]{1,0:T(8,128)S(1)}, f32[8,32]{1,0:T(8,128)S(1)}, u32[]{:S(2)}, u32[]{:S(2)}) collective-permute-start(f32[8,32]{1,0:T(8,128)S(1)} %maximum_select_fusion.1), channel_id=1, source_target_pairs={{0,16},{2,18},{4,20},{6,22},{8,24},{10,26},{12,28},{14,30},{16,0},... | collective-permute-start | bytes 3080 | tf_op jit(solution)/shard_map/ppermute | solution.py:10
  30.4 48.1 %copy-start.91 = (f32[32]{0:T(128)}, f32[32]{0:T(128)S(1)}, u32[]{:S(2)}) copy-start(f32[32]{0:T(128)S(1)} %get-tuple-element.490) | copy-start | bytes 388
  30.7 47.9 %copy-start.95 = (f32[32]{0:T(128)}, f32[32]{0:T(128)S(1)}, u32[]{:S(2)}) copy-start(f32[32]{0:T(128)S(1)} %get-tuple-element.416) | copy-start | bytes 388
  30.7 47.9 %copy-start.97 = (f32[32]{0:T(128)}, f32[32]{0:T(128)S(1)}, u32[]{:S(2)}) copy-start(f32[32]{0:T(128)S(1)} %get-tuple-element.488) | copy-start | bytes 388
  35.4 2.3 collective-permute-start.5
  35.4 29.7 %copy-start.5 = (f32[32,128,64]{1,2,0:T(8,128)S(1)}, f32[32,128,64]{1,2,0:T(8,128)}, u32[]{:S(2)}) copy-start(f32[32,128,64]{1,2,0:T(8,128)} %get-tuple-element.467) | copy-start | bytes 3145732
  39.0 26.2 %collective-permute-start.6 = (f32[16,128,64]{1,2,0:T(8,128)S(1)}, f32[16,128,64]{1,2,0:T(8,128)S(1)}, u32[]{:S(2)}, u32[]{:S(2)}) collective-permute-start(f32[16,128,64]{1,2,0:T(8,128)S(1)} %dynamic-slice_add_fusion.2), channel_id=1, source_target_pairs={{0,16},{2,18},{4,20},{6,22},{8,24},{10,26},{12,28},{14,30},{16,0},... | collective-permute-start | bytes 1572872 | tf_op jit(solution)/shard_map/ppermute | solution.py:10
  41.6 27.8 %copy-start.87 = (f32[32]{0:T(128)}, f32[32]{0:T(128)S(1)}, u32[]{:S(2)}) copy-start(f32[32]{0:T(128)S(1)} %exp.162) | copy-start | bytes 388
  41.6 27.8 %copy-start.85 = (f32[32]{0:T(128)}, f32[32]{0:T(128)S(1)}, u32[]{:S(2)}) copy-start(f32[32]{0:T(128)S(1)} %exp.163) | copy-start | bytes 388
  41.7 27.7 %copy-start.104 = (f32[32]{0:T(128)}, f32[32]{0:T(128)S(1)}, u32[]{:S(2)}) copy-start(f32[32]{0:T(128)S(1)} %exp.170) | copy-start | bytes 388
  43.3 39.5 %copy-start = (f32[32,128,64]{1,2,0:T(8,128)}, f32[32,128,64]{1,2,0:T(8,128)S(1)}, u32[]{:S(2)}) copy-start(f32[32,128,64]{1,2,0:T(8,128)S(1)} %add_select_fusion.6) | copy-start | bytes 3145732
  65.3 13.3 %collective-permute-start.7 = (f32[16,128,64]{1,2,0:T(8,128)S(1)}, f32[16,128,64]{1,2,0:T(8,128)}, u32[]{:S(2)}, u32[]{:S(2)}) collective-permute-start(f32[16,128,64]{1,2,0:T(8,128)S(1)} %constant_dynamic-slice_fusion.8), channel_id=1, source_target_pairs={{0,4},{2,6},{4,0},{6,2},{8,12},{10,14},{12,8},{14,10},{16,20},{18,... | collective-permute-start | bytes 1572872 | tf_op jit(solution)/shard_map/ppermute | solution.py:10
  71.2 7.4 %collective-permute-start.9 = (f32[16,128,64]{1,2,0:T(8,128)}, f32[16,128,64]{1,2,0:T(8,128)}, u32[]{:S(2)}, u32[]{:S(2)}) collective-permute-start(f32[16,128,64]{1,2,0:T(8,128)} %constant_dynamic-slice_fusion.7), channel_id=1, source_target_pairs={{0,2},{2,0},{4,6},{6,4},{8,10},{10,8},{12,14},{14,12},{16,18},{18,... | collective-permute-start | bytes 1572872 | tf_op jit(solution)/shard_map/ppermute | solution.py:10
  78.6 2.9 %collective-permute-start.8 = (f32[16,128,64]{1,2,0:T(8,128)}, f32[16,128,64]{1,2,0:T(8,128)}, u32[]{:S(2)}, u32[]{:S(2)}) collective-permute-start(f32[16,128,64]{1,2,0:T(8,128)} %collective-permute-done.7), channel_id=1, source_target_pairs={{0,2},{2,0},{4,6},{6,4},{8,10},{10,8},{12,14},{14,12},{16,18},{18,... | collective-permute-start | bytes 1572872 | tf_op jit(solution)/shard_map/ppermute | solution.py:10
  80.0 14.4 %collective-permute-start.10 = (f32[16,128,64]{1,2,0:T(8,128)S(1)}, f32[16,128,64]{1,2,0:T(8,128)S(1)}, u32[]{:S(2)}, u32[]{:S(2)}) collective-permute-start(f32[16,128,64]{1,2,0:T(8,128)S(1)} %dynamic-slice_add_fusion.1), channel_id=1, source_target_pairs={{0,8},{2,10},{4,12},{6,14},{8,0},{10,2},{12,4},{14,6},{16,24},{18,... | collective-permute-start | bytes 1572872 | tf_op jit(solution)/shard_map/ppermute | solution.py:10
  94.6 13.6 %collective-permute-start.11 = (f32[16,128,64]{1,2,0:T(8,128)S(1)}, f32[16,128,64]{1,2,0:T(8,128)}, u32[]{:S(2)}, u32[]{:S(2)}) collective-permute-start(f32[16,128,64]{1,2,0:T(8,128)S(1)} %constant_dynamic-slice_fusion.6), channel_id=1, source_target_pairs={{0,8},{2,10},{4,12},{6,14},{8,0},{10,2},{12,4},{14,6},{16,24},{18,... | collective-permute-start | bytes 1572872 | tf_op jit(solution)/shard_map/ppermute | solution.py:10
  99.4 10.2 %collective-permute-start.13 = (f32[16,128,64]{1,2,0:T(8,128)}, f32[16,128,64]{1,2,0:T(8,128)}, u32[]{:S(2)}, u32[]{:S(2)}) collective-permute-start(f32[16,128,64]{1,2,0:T(8,128)} %constant_dynamic-slice_fusion.4), channel_id=1, source_target_pairs={{0,2},{2,0},{4,6},{6,4},{8,10},{10,8},{12,14},{14,12},{16,18},{18,... | collective-permute-start | bytes 1572872 | tf_op jit(solution)/shard_map/ppermute | solution.py:10
  108.2 4.3 %collective-permute-start.12 = (f32[16,128,64]{1,2,0:T(8,128)}, f32[16,128,64]{1,2,0:T(8,128)}, u32[]{:S(2)}, u32[]{:S(2)}) collective-permute-start(f32[16,128,64]{1,2,0:T(8,128)} %collective-permute-done.11), channel_id=1, source_target_pairs={{0,2},{2,0},{4,6},{6,4},{8,10},{10,8},{12,14},{14,12},{16,18},{18,... | collective-permute-start | bytes 1572872 | tf_op jit(solution)/shard_map/ppermute | solution.py:10
  110.9 14.4 %collective-permute-start.14 = (f32[16,128,64]{1,2,0:T(8,128)S(1)}, f32[16,128,64]{1,2,0:T(8,128)S(1)}, u32[]{:S(2)}, u32[]{:S(2)}) collective-permute-start(f32[16,128,64]{1,2,0:T(8,128)S(1)} %dynamic-slice_add_fusion), channel_id=1, source_target_pairs={{0,4},{2,6},{4,0},{6,2},{8,12},{10,14},{12,8},{14,10},{16,20},{18,... | collective-permute-start | bytes 1572872 | tf_op jit(solution)/shard_map/ppermute | solution.py:10
  126.3 77.6 %collective-permute-start.17 = (f32[16,128,64]{1,2,0:T(8,128)}, f32[16,128,64]{1,2,0:T(8,128)}, u32[]{:S(2)}, u32[]{:S(2)}) collective-permute-start(f32[16,128,64]{1,2,0:T(8,128)} %constant_dynamic-slice_fusion.3), channel_id=1, source_target_pairs={{0,16},{2,18},{4,20},{6,22},{8,24},{10,26},{12,28},{14,30},{16,0},... | collective-permute-start | bytes 1572872 | tf_op jit(solution)/shard_map/ppermute | solution.py:10
  203.9 9.7 %collective-permute-start.18 = (f32[16,128,64]{1,2,0:T(8,128)}, f32[16,128,64]{1,2,0:T(8,128)}, u32[]{:S(2)}, u32[]{:S(2)}) collective-permute-start(f32[16,128,64]{1,2,0:T(8,128)} %collective-permute-done.17), channel_id=1, source_target_pairs={{0,2},{2,0},{4,6},{6,4},{8,10},{10,8},{12,14},{14,12},{16,18},{18,... | collective-permute-start | bytes 1572872 | tf_op jit(solution)/shard_map/ppermute | solution.py:10
  235.0 7.4 %collective-permute-start.19 = (f32[16,32]{1,0:T(8,128)S(1)}, f32[16,32]{1,0:T(8,128)S(1)}, u32[]{:S(2)}, u32[]{:S(2)}) collective-permute-start(f32[16,32]{1,0:T(8,128)S(1)} %select_add_fusion), channel_id=1, source_target_pairs={{0,2},{2,0},{4,6},{6,4},{8,10},{10,8},{12,14},{14,12},{16,18},{18,... | collective-permute-start | bytes 6152 | tf_op jit(solution)/shard_map/ppermute | solution.py:10
  235.6 16.0 %collective-permute-start.15 = (f32[32,128,64]{1,2,0:T(8,128)}, f32[32,128,64]{1,2,0:T(8,128)}, u32[]{:S(2)}, u32[]{:S(2)}) collective-permute-start(f32[32,128,64]{1,2,0:T(8,128)} %get-tuple-element.454), channel_id=1, source_target_pairs={{0,2},{2,0},{4,6},{6,4},{8,10},{10,8},{12,14},{14,12},{16,18},{18,... | collective-permute-start | bytes 3145736 | tf_op jit(solution)/shard_map/ppermute | solution.py:10
  242.8 3.7 %collective-permute-start.20 = (f32[16,32]{1,0:T(8,128)S(1)}, f32[16,32]{1,0:T(8,128)S(1)}, u32[]{:S(2)}, u32[]{:S(2)}) collective-permute-start(f32[16,32]{1,0:T(8,128)S(1)} %fusion.128), channel_id=1, source_target_pairs={{0,4},{2,6},{4,0},{6,2},{8,12},{10,14},{12,8},{14,10},{16,20},{18,... | collective-permute-start | bytes 6152 | tf_op jit(solution)/shard_map/ppermute | solution.py:10
  247.4 4.1 %collective-permute-start.21 = (f32[16,32]{1,0:T(8,128)S(1)}, f32[16,32]{1,0:T(8,128)S(1)}, u32[]{:S(2)}, u32[]{:S(2)}) collective-permute-start(f32[16,32]{1,0:T(8,128)S(1)} %fusion.129), channel_id=1, source_target_pairs={{0,8},{2,10},{4,12},{6,14},{8,0},{10,2},{12,4},{14,6},{16,24},{18,... | collective-permute-start | bytes 6152 | tf_op jit(solution)/shard_map/ppermute | solution.py:10
  251.5 9.9 %collective-permute-start.22 = (f32[16,32]{1,0:T(8,128)S(1)}, f32[16,32]{1,0:T(8,128)S(1)}, u32[]{:S(2)}, u32[]{:S(2)}) collective-permute-start(f32[16,32]{1,0:T(8,128)S(1)} %add.279), channel_id=1, source_target_pairs={{0,16},{2,18},{4,20},{6,22},{8,24},{10,26},{12,28},{14,30},{16,0},... | collective-permute-start | bytes 6152 | tf_op jit(solution)/shard_map/ppermute | solution.py:10
  259.1 12.9 %collective-permute-start.16 = (bf16[128,2048]{1,0:T(8,128)(2,1)S(1)}, bf16[128,2048]{1,0:T(8,128)(2,1)S(1)}, u32[]{:S(2)}, u32[]{:S(2)}) collective-permute-start(bf16[128,2048]{1,0:T(8,128)(2,1)S(1)} %add_convert_fusion), channel_id=1, source_target_pairs={{1,0},{0,1},{3,2},{2,3},{5,4},{4,5},{7,6},{6,7},{9,8},{8,9},{11,10... | collective-permute-start | bytes 1572872 | tf_op jit(solution)/shard_map/ppermute | solution.py:16
  (109 other events, 1116.1 us)
